TPU v7x, 512 devices: a whole 4x8x8 slice. The times are simulated.
512 devices in a mesh: seq: 128 (over y, z, core), sub: 4 (over x).
Axes of the slice: x: 4, y: 8, z: 8, core: 2. Of those that a mesh axis runs over, the one named last changes fastest.
Arguments:
- linear_query: bfloat16 [32768, 256], P(('seq', 'sub')), may hold values from -6 to 6
- linear_key: bfloat16 [32768, 256], P(('seq', 'sub')), may hold values from -6 to 6
- linear_value: bfloat16 [32768, 2048], P(('seq', 'sub')), may hold values from -6 to 6
- lin_gain: float32 [2048], replicated, may hold values from 0.1 to 1.9
- window_query: bfloat16 [32768, 2048], P(('seq', 'sub')), may hold values from -6 to 6
- window_key: bfloat16 [32768, 2048], P(('seq', 'sub')), may hold values from -6 to 6
- window_value: bfloat16 [32768, 2048], P(('seq', 'sub')), may hold values from -6 to 6
Outputs:
- linear_out: bfloat16 [32768, 2048], P(('seq', 'sub'))
- window_out: bfloat16 [32768, 2048], P(('seq', 'sub'))
All inputs are finite; a program needn't handle non-finite values.
Results may differ from a plain program's by a relative error of at most 0.007.
Values may be sent and summed in bfloat16 or wider, within the bound.
No kernel may reach another device: no remote copies, remote signals or barrier semaphores. Data moves between devices by JAX's collectives and lax.ppermute only.
A program may use at most 128 MiB of HBM per device.

v0:
```python
import math
import jax
import jax.numpy as jnp
import numpy as np
from jax import lax
from jax.sharding import Mesh
from jax.sharding import PartitionSpec as P

FDIM = 16
VDIM = 128
SDIM = 128
WINDOW = 512
CORES = 2
FEAT_PAD = 160
ALL = ("y", "z", "core", "sub")
GROUP = ("core", "sub")


def pair_tables(for_query):
    pairs = [(0, 0)] + [(0, a + 1) for a in range(FDIM)]
    pairs += [(a + 1, b + 1) for a in range(FDIM) for b in range(a, FDIM)]
    first = np.zeros((FDIM + 1, FEAT_PAD), np.float32)
    second = np.zeros((FDIM + 1, FEAT_PAD), np.float32)
    for f, (a, b) in enumerate(pairs):
        first[a, f] = 0.5 if for_query and a == b and (a > 0) else 1.0
        second[b, f] = 1.0
    return (first, second)


def passed_along(shard, axis, by):
    size = lax.axis_size(axis)
    pairs = [(i, i + by) for i in range(size) if 0 <= i + by < size]
    return lax.ppermute(shard, axis, pairs)


def sym_features(vectors, for_query):
    halved = vectors * 0.5
    ext = jnp.concatenate([jnp.ones(halved.shape[:-1] + (1,), jnp.float32), halved], axis=-1)
    first, second = pair_tables(for_query)
    pick = lambda table: jnp.einsum(
        "jhi,if->jhf", ext, jnp.asarray(table), precision=lax.Precision.HIGHEST
    )
    return pick(first) * pick(second)


def groups_before(total):
    z_count = lax.axis_size("z")
    heads, feats, width = total.shape
    dealt = total.reshape(heads, z_count, feats // z_count, width)
    held = lax.all_to_all(dealt, "z", split_axis=1, concat_axis=1, tiled=True)
    running = jnp.cumsum(held, axis=1)
    line_total = running[:, -1]
    along_y = lax.all_gather(line_total, "y")
    y_before = jnp.arange(along_y.shape[0]) < lax.axis_index("y")
    lines_before = jnp.sum(jnp.where(y_before[:, None, None, None], along_y, 0.0), axis=0)
    prefix = running - held + lines_before[:, None]
    back = lax.all_to_all(prefix, "z", split_axis=1, concat_axis=1, tiled=True)
    return back.reshape(heads, feats, width)


def linear_heads(linear_query, linear_key, linear_value, lin_gain):
    rows_dev = linear_query.shape[0]
    group_count = lax.axis_size(GROUP)
    lin_heads = linear_query.shape[1] // FDIM
    own_heads = lin_heads // group_count
    packed = jnp.concatenate(
        [
            linear_query.reshape(rows_dev, group_count, own_heads * FDIM),
            linear_key.reshape(rows_dev, group_count, own_heads * FDIM),
            linear_value.reshape(rows_dev, group_count, own_heads * VDIM),
        ],
        axis=-1,
    )
    got = lax.all_to_all(packed, GROUP, split_axis=1, concat_axis=0, tiled=True)
    rows = got.shape[0]
    got = got.reshape(rows, -1)
    query_bf = got[:, : own_heads * FDIM].reshape(rows, own_heads, FDIM)
    key_bf = got[:, own_heads * FDIM : 2 * own_heads * FDIM].reshape(rows, own_heads, FDIM)
    value_lin = got[:, 2 * own_heads * FDIM :].reshape(rows, own_heads, VDIM).astype(jnp.float32)
    query_lin = query_bf.astype(jnp.float32)
    key_lin = key_bf.astype(jnp.float32)
    total = jnp.einsum(
        "jhf,jhe->hfe", sym_features(key_lin, False), value_lin, precision=lax.Precision.HIGHEST
    )
    before = groups_before(total)
    from_state = jnp.einsum(
        "ihf,hfe->ihe", sym_features(query_lin, True), before, precision=lax.Precision.HIGHEST
    )
    dot_inner = (
        jnp.einsum("ihd,jhd->hij", query_bf, key_bf, preferred_element_type=jnp.float32) * 0.25
    )
    weight = 1.0 + dot_inner + 0.5 * dot_inner * dot_inner
    causal = (
        jnp.arange(rows, dtype=jnp.int32)[:, None] >= jnp.arange(rows, dtype=jnp.int32)[None, :]
    )
    weight = jnp.where(causal[None], weight, jnp.float32(0.0))
    local_sum = jnp.einsum("hij,jhe->ihe", weight, value_lin, precision=lax.Precision.HIGHEST)
    numerator = local_sum + from_state
    inv_rms = lax.rsqrt(jnp.mean(numerator * numerator, axis=-1, keepdims=True) + 1e-05)
    gain_rows = lax.dynamic_slice_in_dim(
        lin_gain.reshape(lin_heads, VDIM), lax.axis_index(GROUP) * own_heads, own_heads, 0
    )
    out = (numerator * inv_rms * gain_rows).astype(jnp.bfloat16)
    out = out.reshape(group_count, rows_dev, own_heads * VDIM)
    back = lax.all_to_all(out, GROUP, split_axis=0, concat_axis=2, tiled=True)
    return back.reshape(rows_dev, lin_heads * VDIM)


def shards(
    linear_query, linear_key, linear_value, lin_gain, window_query, window_key, window_value
):
    rows_dev = linear_query.shape[0]
    dev_count = lax.axis_size(ALL)
    group_count = lax.axis_size(GROUP)
    device_pos = lax.axis_index(ALL)
    base_row = device_pos * rows_dev
    reach_dev = WINDOW // rows_dev
    channels = window_key.shape[1]
    head_count = channels // SDIM
    lin_heads = linear_query.shape[1] // FDIM
    stacked = jnp.stack([window_key, window_value])
    earlier = [passed_along(stacked, ALL, reach_dev - t) for t in range(reach_dev)]
    earlier = jnp.concatenate(earlier, axis=1)
    key_rows = jnp.concatenate([earlier[0], window_key], axis=0).reshape(-1, head_count, SDIM)
    value_rows = jnp.concatenate([earlier[1], window_value], axis=0).reshape(-1, head_count, SDIM)
    query_heads = window_query.reshape(rows_dev, head_count, SDIM)
    scores = jnp.einsum(
        "ihd,jhd->hij", query_heads, key_rows, preferred_element_type=jnp.float32
    ) * (1.0 / math.sqrt(SDIM))
    query_pos = base_row + jnp.arange(rows_dev, dtype=jnp.int32)
    key_pos = (
        base_row - reach_dev * rows_dev + jnp.arange((reach_dev + 1) * rows_dev, dtype=jnp.int32)
    )
    allowed = (
        (key_pos[None, :] <= query_pos[:, None])
        & (key_pos[None, :] > query_pos[:, None] - WINDOW)
        & (key_pos[None, :] >= 0)
    )
    scores = jnp.where(allowed[None], scores, jnp.float32(-1e30))
    row_max = jnp.max(scores, axis=-1, keepdims=True)
    exp_scores = jnp.exp(scores - row_max)
    weights_bf = (exp_scores / jnp.sum(exp_scores, axis=-1, keepdims=True)).astype(jnp.bfloat16)
    mixed = jnp.einsum("hij,jhd->ihd", weights_bf, value_rows, preferred_element_type=jnp.float32)
    window_out = mixed.reshape(rows_dev, channels).astype(jnp.bfloat16)
    linear_out = linear_heads(linear_query, linear_key, linear_value, lin_gain)
    return (linear_out, window_out)


def solution(mesh):
    seq_count = mesh.shape["seq"]
    sub_count = mesh.shape["sub"]
    lines = seq_count // CORES
    z_count = math.isqrt(lines)
    split_mesh = Mesh(
        np.asarray(mesh.devices).reshape(lines // z_count, z_count, CORES, sub_count), ALL
    )
    rows = P(ALL, None)
    in_specs = (rows, rows, rows, P(), rows, rows, rows)
    out_specs = (rows, rows)
    return jax.shard_map(
        shards, mesh=split_mesh, in_specs=in_specs, out_specs=out_specs, check_vma=False
    )
```

profile of v0, /device:TPU:1, one launch (start us, length us, event | category | flops | bytes accessed | tf_op | source)
XLA Modules:
  0.0 187.4 jit_solution(14541325597579867296)
XLA Ops:
  0.7 2.0 %pad_maximum_fusion = bf16[2,64,2048]{2,1,0:T(8,128)(2,1)} fusion(bf16[1,64,2048]{2,1,0:T(8,128)(2,1)} %bitcast.96, bf16[1,64,2048]{2,1,0:T(8,128)(2,1)} %bitcast.95), kind=kLoop, calls=%fused_computation.35 | loop fusion | flops 262144 | bytes 1048576 | tf_op jit(solution)/shard_map/stack | solution.py:121
  2.7 4.8 %collective-permute-start = (bf16[2,64,2048]{2,1,0:T(8,128)(2,1)}, bf16[2,64,2048]{2,1,0:T(8,128)(2,1)S(1)}, u32[]{:S(2)}, u32[]{:S(2)}) collective-permute-start(bf16[2,64,2048]{2,1,0:T(8,128)(2,1)} %pad_maximum_fusion), channel_id=1, source_target_pairs={{0,8},{1,9},{2,10},{3,11},{4,12},{5,13},{6,14},{7,15},{8,16},{9,17... | collective-permute-start | bytes 1572872 | tf_op jit(solution)/shard_map/ppermute | solution.py:33
  7.5 7.0 %collective-permute-start.1 = (bf16[2,64,2048]{2,1,0:T(8,128)(2,1)}, bf16[2,64,2048]{2,1,0:T(8,128)(2,1)S(1)}, u32[]{:S(2)}, u32[]{:S(2)}) collective-permute-start(bf16[2,64,2048]{2,1,0:T(8,128)(2,1)} %pad_maximum_fusion), channel_id=1, source_target_pairs={{0,7},{1,8},{2,9},{3,10},{4,11},{5,12},{6,13},{7,14},{8,15},{9,16}... | collective-permute-start | bytes 1572872 | tf_op jit(solution)/shard_map/ppermute | solution.py:33
  14.6 4.5 %collective-permute-start.2 = (bf16[2,64,2048]{2,1,0:T(8,128)(2,1)}, bf16[2,64,2048]{2,1,0:T(8,128)(2,1)S(1)}, u32[]{:S(2)}, u32[]{:S(2)}) collective-permute-start(bf16[2,64,2048]{2,1,0:T(8,128)(2,1)} %pad_maximum_fusion), channel_id=1, source_target_pairs={{0,6},{1,7},{2,8},{3,9},{4,10},{5,11},{6,12},{7,13},{8,14},{9,15},... | collective-permute-start | bytes 1572872 | tf_op jit(solution)/shard_map/ppermute | solution.py:33
  19.1 2.5 %collective-permute-start.3 = (bf16[2,64,2048]{2,1,0:T(8,128)(2,1)}, bf16[2,64,2048]{2,1,0:T(8,128)(2,1)}, u32[]{:S(2)}, u32[]{:S(2)}) collective-permute-start(bf16[2,64,2048]{2,1,0:T(8,128)(2,1)} %pad_maximum_fusion), channel_id=1, source_target_pairs={{0,5},{1,6},{2,7},{3,8},{4,9},{5,10},{6,11},{7,12},{8,13},{9,14},{... | collective-permute-start | bytes 1572872 | tf_op jit(solution)/shard_map/ppermute | solution.py:33
  21.6 5.5 %collective-permute-start.4 = (bf16[2,64,2048]{2,1,0:T(8,128)(2,1)}, bf16[2,64,2048]{2,1,0:T(8,128)(2,1)}, u32[]{:S(2)}, u32[]{:S(2)}) collective-permute-start(bf16[2,64,2048]{2,1,0:T(8,128)(2,1)} %pad_maximum_fusion), channel_id=1, source_target_pairs={{0,4},{1,5},{2,6},{3,7},{4,8},{5,9},{6,10},{7,11},{8,12},{9,13},{1... | collective-permute-start | bytes 1572872 | tf_op jit(solution)/shard_map/ppermute | solution.py:33
  31.1 4.5 %all-to-all-start = ((bf16[64,8,320]{2,0,1:T(8,128)(2,1)}), bf16[64,8,320]{2,0,1:T(8,128)(2,1)S(1)}, u32[]{:S(2)}, u32[]{:S(2)}) async-start(bf16[64,8,320]{2,0,1:T(8,128)(2,1)} %pad_maximum_fusion.1), calls=%async_computation | async-start | bytes 786432 | tf_op jit(solution)/shard_map/all_to_all | solution.py:74
  38.1 5.5 %all-to-all-done = bf16[64,8,320]{2,0,1:T(8,128)(2,1)S(1)} async-done(((bf16[64,8,320]{2,0,1:T(8,128)(2,1)}), bf16[64,8,320]{2,0,1:T(8,128)(2,1)S(1)}, u32[]{:S(2)}, u32[]{:S(2)}) %all-to-all-start) | async-done | bytes 327712 | tf_op jit(solution)/shard_map/all_to_all | solution.py:74
  46.8 25.6 %all-to-all-start.1 = ((f32[2,8,20,128]{3,0,2,1:T(2,128)}), f32[2,8,20,128]{3,0,2,1:T(2,128)}, u32[]{:S(2)}, u32[]{:S(2)}) async-start(f32[2,8,20,128]{3,0,2,1:T(2,128)} %bitcast.12), calls=%async_computation.1 | async-start | bytes 327680 | tf_op jit(solution)/shard_map/all_to_all | solution.py:50
  73.8 1.9 %collective-permute-start.5 = (bf16[2,64,2048]{2,1,0:T(8,128)(2,1)}, bf16[2,64,2048]{2,1,0:T(8,128)(2,1)}, u32[]{:S(2)}, u32[]{:S(2)}) collective-permute-start(bf16[2,64,2048]{2,1,0:T(8,128)(2,1)} %pad_maximum_fusion), channel_id=1, source_target_pairs={{0,3},{1,4},{2,5},{3,6},{4,7},{5,8},{6,9},{7,10},{8,11},{9,12},{10... | collective-permute-start | bytes 1572872 | tf_op jit(solution)/shard_map/ppermute | solution.py:33
  75.7 1.9 %collective-permute-start.6 = (bf16[2,64,2048]{2,1,0:T(8,128)(2,1)}, bf16[2,64,2048]{2,1,0:T(8,128)(2,1)}, u32[]{:S(2)}, u32[]{:S(2)}) collective-permute-start(bf16[2,64,2048]{2,1,0:T(8,128)(2,1)} %pad_maximum_fusion), channel_id=1, source_target_pairs={{0,2},{1,3},{2,4},{3,5},{4,6},{5,7},{6,8},{7,9},{8,10},{9,11},{10,... | collective-permute-start | bytes 1572872 | tf_op jit(solution)/shard_map/ppermute | solution.py:33
  77.6 5.4 %collective-permute-start.7 = (bf16[2,64,2048]{2,1,0:T(8,128)(2,1)}, bf16[2,64,2048]{2,1,0:T(8,128)(2,1)}, u32[]{:S(2)}, u32[]{:S(2)}) collective-permute-start(bf16[2,64,2048]{2,1,0:T(8,128)(2,1)} %pad_maximum_fusion), channel_id=1, source_target_pairs={{0,1},{1,2},{2,3},{3,4},{4,5},{5,6},{6,7},{7,8},{8,9},{9,10},{10,1... | collective-permute-start | bytes 1572872 | tf_op jit(solution)/shard_map/ppermute | solution.py:33
  84.6 2.6 %fusion.9 = f32[2,128,512]{2,1,0:T(8,128)} fusion(bf16[512,2,128]{0,2,1:T(8,128)(2,1)S(1)} %bitcast.98, f32[2,512,512]{2,1,0:T(8,128)S(1)} %fusion.75, pred[512,512]{1,0:T(8,128)(4,1)S(1)} %iota_compare_fusion), kind=kOutput, calls=%fused_computation.12 | convolution fusion | flops 808452096 | bytes 3145728 | tf_op jit(solution)/shard_map/hij,jhe->ihe/dot_general | solution.py:97
  89.7 2.4 %copy.104 = bf16[2,64,2048]{1,2,0:T(8,128)(2,1)} copy(bf16[2,64,2048]{2,1,0:T(8,128)(2,1)} %collective-permute-done.3) | data formatting | bytes 1048576 | tf_op jit(solution)/shard_map/ppermute | solution.py:33
  92.0 2.4 %copy.105 = bf16[2,64,2048]{1,2,0:T(8,128)(2,1)} copy(bf16[2,64,2048]{2,1,0:T(8,128)(2,1)} %collective-permute-done.4) | data formatting | bytes 1048576 | tf_op jit(solution)/shard_map/ppermute | solution.py:33
  94.4 3.7 %collective-permute-done.5 = bf16[2,64,2048]{2,1,0:T(8,128)(2,1)} collective-permute-done((bf16[2,64,2048]{2,1,0:T(8,128)(2,1)}, bf16[2,64,2048]{2,1,0:T(8,128)(2,1)}, u32[]{:S(2)}, u32[]{:S(2)}) %collective-permute-start.5) | collective-permute-done | bytes 524320 | tf_op jit(solution)/shard_map/ppermute | solution.py:33
  98.1 2.4 %copy.106 = bf16[2,64,2048]{1,2,0:T(8,128)(2,1)} copy(bf16[2,64,2048]{2,1,0:T(8,128)(2,1)} %collective-permute-done.5) | data formatting | bytes 1048576 | tf_op jit(solution)/shard_map/ppermute | solution.py:33
  100.5 2.4 %copy.107 = bf16[2,64,2048]{1,2,0:T(8,128)(2,1)} copy(bf16[2,64,2048]{2,1,0:T(8,128)(2,1)} %collective-permute-done.6) | data formatting | bytes 1048576 | tf_op jit(solution)/shard_map/ppermute | solution.py:33
  103.0 2.4 %copy.108 = bf16[2,64,2048]{1,2,0:T(8,128)(2,1)} copy(bf16[2,64,2048]{2,1,0:T(8,128)(2,1)} %collective-permute-done.7) | data formatting | bytes 1048576 | tf_op jit(solution)/shard_map/ppermute | solution.py:33
  105.4 10.8 %concatenate.31 = bf16[2,512,2048]{1,2,0:T(8,128)(2,1)} concatenate(bf16[2,64,2048]{1,2,0:T(8,128)(2,1)S(1)} %copy.101, bf16[2,64,2048]{1,2,0:T(8,128)(2,1)S(1)} %copy.102, bf16[2,64,2048]{1,2,0:T(8,128)(2,1)S(1)} %copy.103, bf16[2,64,2048]{1,2,0:T(8,128)(2,1)} %copy.104, bf16[2,64,2048]{1,2,0:T(8,128)(2,1)} %copy.105, bf16[2,64,2048]{1,2,0:T(8,128)(2,1)} %copy.106, ...), dimensions={1} | concatenate | bytes 8388608 | tf_op jit(solution)/shard_map/concatenate | solution.py:123
  116.1 3.9 %fusion.67 = (bf16[1,512,2048]{1,2,0:T(8,128)(2,1)}, bf16[1,512,2048]{1,2,0:T(8,128)(2,1)S(1)}) fusion(bf16[2,512,2048]{1,2,0:T(8,128)(2,1)} %concatenate.31), kind=kLoop, calls=%fused_computation.77 | loop fusion | bytes 8388608 | tf_op jit(solution)/shard_map/slice | solution.py:124
  120.0 3.9 %copy.111 = bf16[512,16,128]{2,0,1:T(8,128)(2,1)} copy(bf16[512,16,128]{0,2,1:T(8,128)(2,1)} %bitcast.90) | data formatting | bytes 4194304 | tf_op jit(solution)/shard_map/concatenate | solution.py:124
  124.0 2.4 %copy.109 = bf16[512,16,128]{2,0,1:T(8,128)(2,1)} copy(bf16[512,16,128]{0,2,1:T(8,128)(2,1)S(1)} %bitcast.89) | data formatting | bytes 4194304 | tf_op jit(solution)/shard_map/concatenate | solution.py:125
  127.3 22.0 %all-gather = f32[16,1,20,128]{3,1,2,0:T(1,128)S(1)} all-gather(f32[2,1,20,128]{3,1,2,0:T(1,128)S(1)} %copy.96), channel_id=2, replica_groups=mesh['y'=8,'z'=8,'core'=2,'sub'=4] {'y'}, dimensions={0}, use_global_device_ids=true | all-gather | bytes 184320 | tf_op jit(solution)/shard_map/all_gather | solution.py:53
  149.5 1.6 subtract_add_fusion
  151.1 6.7 %all-to-all-start.2 = ((f32[2,8,20,128]{3,0,2,1:T(2,128)}), f32[2,8,20,128]{3,0,2,1:T(2,128)S(1)}, u32[]{:S(2)}, u32[]{:S(2)}) async-start(f32[2,8,20,128]{3,0,2,1:T(2,128)} %bitcast.88), calls=%async_computation.2 | async-start | bytes 327680 | tf_op jit(solution)/shard_map/all_to_all | solution.py:57
  157.9 4.3 %fusion.69 = (f32[16,64]{1,0:T(8,128)S(1)}, f32[16,64,576]{2,1,0:T(8,128)}) fusion(pred[64,576]{1,0:T(8,128)(4,1)S(1)} %and_and_fusion, bf16[64,16,128]{2,0,1:T(8,128)(2,1)S(1)} %copy-done.7, bf16[512,16,128]{2,0,1:T(8,128)(2,1)} %copy.111, bf16[64,2048]{1,0:T(8,128)(2,1)S(1)} %copy-done), kind=kOutput, calls=%fused_computation.79 | convolution fusion | flops 158073408 | bytes 5021696 | tf_op jit(solution)/shard_map/sub | solution.py:141
  162.2 4.1 %all-to-all-done.2 = f32[2,8,20,128]{3,0,2,1:T(2,128)S(1)} async-done(((f32[2,8,20,128]{3,0,2,1:T(2,128)}), f32[2,8,20,128]{3,0,2,1:T(2,128)S(1)}, u32[]{:S(2)}, u32[]{:S(2)}) %all-to-all-start.2) | async-done | bytes 163872 | tf_op jit(solution)/shard_map/all_to_all | solution.py:57
  166.3 1.8 multiply_reduce_fusion
  169.2 10.9 %all-to-all-start.3 = ((bf16[8,64,256]{2,1,0:T(8,128)(2,1)}), bf16[8,64,256]{2,1,0:T(8,128)(2,1)S(1)}, u32[]{:S(2)}, u32[]{:S(2)}) async-start(bf16[8,64,256]{2,1,0:T(8,128)(2,1)} %reshape.179), calls=%async_computation.3 | async-start | bytes 524288 | tf_op jit(solution)/shard_map/all_to_all | solution.py:105
  180.2 2.4 %fusion.24 = bf16[16,8,8,128]{3,2,1,0:T(8,128)(2,1)S(1)} fusion(bf16[64,16,128]{2,0,1:T(8,128)(2,1)S(1)} %copy-done.6, bf16[512,16,128]{2,0,1:T(8,128)(2,1)S(1)} %copy-done.2, f32[16,64,576]{2,1,0:T(8,128)} %get-tuple-element.9, f32[16,64]{1,0:T(8,128)S(1)} %get-tuple-element.8), kind=kOutput, calls=%fused_computation.28 | convolution fusion | flops 157024256 | bytes 4984832 | tf_op jit(solution)/shard_map/hij,jhd->ihd/dot_general | solution.py:143
  183.3 3.4 %all-to-all-done.3 = bf16[8,64,256]{2,1,0:T(8,128)(2,1)S(1)} async-done(((bf16[8,64,256]{2,1,0:T(8,128)(2,1)}), bf16[8,64,256]{2,1,0:T(8,128)(2,1)S(1)}, u32[]{:S(2)}, u32[]{:S(2)}) %all-to-all-start.3) | async-done | bytes 262176 | tf_op jit(solution)/shard_map/all_to_all | solution.py:105
  (73 shorter events, 18.8 us)
Async XLA Ops:
  0.6 157.3 %copy-start = (bf16[64,2048]{1,0:T(8,128)(2,1)S(1)}, bf16[64,2048]{1,0:T(8,128)(2,1)}, u32[]{:S(2)}) copy-start(bf16[64,2048]{1,0:T(8,128)(2,1)} %param.15) | copy-start | bytes 786436
  0.6 35.0 %copy-start.3 = (bf16[64,2048]{1,0:T(8,128)(2,1)S(1)}, bf16[64,2048]{1,0:T(8,128)(2,1)}, u32[]{:S(2)}) copy-start(bf16[64,2048]{1,0:T(8,128)(2,1)} %param.16) | copy-start | bytes 786436
  0.7 36.7 %copy-start.4 = (bf16[64,2048]{1,0:T(8,128)(2,1)S(1)}, bf16[64,2048]{1,0:T(8,128)(2,1)}, u32[]{:S(2)}) copy-start(bf16[64,2048]{1,0:T(8,128)(2,1)} %param.17) | copy-start | bytes 786436
  2.7 71.1 %collective-permute-start = (bf16[2,64,2048]{2,1,0:T(8,128)(2,1)}, bf16[2,64,2048]{2,1,0:T(8,128)(2,1)S(1)}, u32[]{:S(2)}, u32[]{:S(2)}) collective-permute-start(bf16[2,64,2048]{2,1,0:T(8,128)(2,1)} %pad_maximum_fusion), channel_id=1, source_target_pairs={{0,8},{1,9},{2,10},{3,11},{4,12},{5,13},{6,14},{7,15},{8,16},{9,17... | collective-permute-start | bytes 1572872 | tf_op jit(solution)/shard_map/ppermute | solution.py:33
  7.5 68.2 %collective-permute-start.1 = (bf16[2,64,2048]{2,1,0:T(8,128)(2,1)}, bf16[2,64,2048]{2,1,0:T(8,128)(2,1)S(1)}, u32[]{:S(2)}, u32[]{:S(2)}) collective-permute-start(bf16[2,64,2048]{2,1,0:T(8,128)(2,1)} %pad_maximum_fusion), channel_id=1, source_target_pairs={{0,7},{1,8},{2,9},{3,10},{4,11},{5,12},{6,13},{7,14},{8,15},{9,16}... | collective-permute-start | bytes 1572872 | tf_op jit(solution)/shard_map/ppermute | solution.py:33
  14.6 63.1 %collective-permute-start.2 = (bf16[2,64,2048]{2,1,0:T(8,128)(2,1)}, bf16[2,64,2048]{2,1,0:T(8,128)(2,1)S(1)}, u32[]{:S(2)}, u32[]{:S(2)}) collective-permute-start(bf16[2,64,2048]{2,1,0:T(8,128)(2,1)} %pad_maximum_fusion), channel_id=1, source_target_pairs={{0,6},{1,7},{2,8},{3,9},{4,10},{5,11},{6,12},{7,13},{8,14},{9,15},... | collective-permute-start | bytes 1572872 | tf_op jit(solution)/shard_map/ppermute | solution.py:33
  19.1 70.6 %collective-permute-start.3 = (bf16[2,64,2048]{2,1,0:T(8,128)(2,1)}, bf16[2,64,2048]{2,1,0:T(8,128)(2,1)}, u32[]{:S(2)}, u32[]{:S(2)}) collective-permute-start(bf16[2,64,2048]{2,1,0:T(8,128)(2,1)} %pad_maximum_fusion), channel_id=1, source_target_pairs={{0,5},{1,6},{2,7},{3,8},{4,9},{5,10},{6,11},{7,12},{8,13},{9,14},{... | collective-permute-start | bytes 1572872 | tf_op jit(solution)/shard_map/ppermute | solution.py:33
  21.6 70.5 %collective-permute-start.4 = (bf16[2,64,2048]{2,1,0:T(8,128)(2,1)}, bf16[2,64,2048]{2,1,0:T(8,128)(2,1)}, u32[]{:S(2)}, u32[]{:S(2)}) collective-permute-start(bf16[2,64,2048]{2,1,0:T(8,128)(2,1)} %pad_maximum_fusion), channel_id=1, source_target_pairs={{0,4},{1,5},{2,6},{3,7},{4,8},{5,9},{6,10},{7,11},{8,12},{9,13},{1... | collective-permute-start | bytes 1572872 | tf_op jit(solution)/shard_map/ppermute | solution.py:33
  30.1 14.0 %copy-start.10 = (f32[17,160,1]{1,0,2:T(8,128)S(1)}, f32[17,160,1]{1,0,2:T(8,128)}, u32[]{:S(2)}) copy-start(f32[17,160,1]{1,0,2:T(8,128)} %constant.80) | copy-start | bytes 32644
  31.1 13.7 %copy-start.8 = (f32[17,160,1]{1,0,2:T(8,128)S(1)}, f32[17,160,1]{1,0,2:T(8,128)}, u32[]{:S(2)}) copy-start(f32[17,160,1]{1,0,2:T(8,128)} %constant.81) | copy-start | bytes 32644
  31.1 12.5 %all-to-all-start = ((bf16[64,8,320]{2,0,1:T(8,128)(2,1)}), bf16[64,8,320]{2,0,1:T(8,128)(2,1)S(1)}, u32[]{:S(2)}, u32[]{:S(2)}) async-start(bf16[64,8,320]{2,0,1:T(8,128)(2,1)} %pad_maximum_fusion.1), calls=%async_computation | async-start | bytes 786432 | tf_op jit(solution)/shard_map/all_to_all | solution.py:74
  43.9 28.6 %copy-start.9 = (f32[17,160,1]{1,0,2:T(8,128)S(1)}, f32[17,160,1]{1,0,2:T(8,128)}, u32[]{:S(2)}) copy-start(f32[17,160,1]{1,0,2:T(8,128)} %constant.82) | copy-start | bytes 32644
  46.8 79.5 %all-to-all-start.1 = ((f32[2,8,20,128]{3,0,2,1:T(2,128)}), f32[2,8,20,128]{3,0,2,1:T(2,128)}, u32[]{:S(2)}, u32[]{:S(2)}) async-start(f32[2,8,20,128]{3,0,2,1:T(2,128)} %bitcast.12), calls=%async_computation.1 | async-start | bytes 327680 | tf_op jit(solution)/shard_map/all_to_all | solution.py:50
  73.8 24.4 %collective-permute-start.5 = (bf16[2,64,2048]{2,1,0:T(8,128)(2,1)}, bf16[2,64,2048]{2,1,0:T(8,128)(2,1)}, u32[]{:S(2)}, u32[]{:S(2)}) collective-permute-start(bf16[2,64,2048]{2,1,0:T(8,128)(2,1)} %pad_maximum_fusion), channel_id=1, source_target_pairs={{0,3},{1,4},{2,5},{3,6},{4,7},{5,8},{6,9},{7,10},{8,11},{9,12},{10... | collective-permute-start | bytes 1572872 | tf_op jit(solution)/shard_map/ppermute | solution.py:33
  75.7 24.8 %collective-permute-start.6 = (bf16[2,64,2048]{2,1,0:T(8,128)(2,1)}, bf16[2,64,2048]{2,1,0:T(8,128)(2,1)}, u32[]{:S(2)}, u32[]{:S(2)}) collective-permute-start(bf16[2,64,2048]{2,1,0:T(8,128)(2,1)} %pad_maximum_fusion), channel_id=1, source_target_pairs={{0,2},{1,3},{2,4},{3,5},{4,6},{5,7},{6,8},{7,9},{8,10},{9,11},{10,... | collective-permute-start | bytes 1572872 | tf_op jit(solution)/shard_map/ppermute | solution.py:33
  77.6 9.5 %copy-start.5 = (bf16[2,64,2048]{2,1,0:T(8,128)(2,1)}, bf16[2,64,2048]{2,1,0:T(8,128)(2,1)S(1)}, u32[]{:S(2)}) copy-start(bf16[2,64,2048]{2,1,0:T(8,128)(2,1)S(1)} %collective-permute-done.2) | copy-start | bytes 1572868
  77.6 25.3 %collective-permute-start.7 = (bf16[2,64,2048]{2,1,0:T(8,128)(2,1)}, bf16[2,64,2048]{2,1,0:T(8,128)(2,1)}, u32[]{:S(2)}, u32[]{:S(2)}) collective-permute-start(bf16[2,64,2048]{2,1,0:T(8,128)(2,1)} %pad_maximum_fusion), channel_id=1, source_target_pairs={{0,1},{1,2},{2,3},{3,4},{4,5},{5,6},{6,7},{7,8},{8,9},{9,10},{10,1... | collective-permute-start | bytes 1572872 | tf_op jit(solution)/shard_map/ppermute | solution.py:33
  123.9 33.9 %copy-start.7 = (bf16[64,16,128]{2,0,1:T(8,128)(2,1)S(1)}, bf16[64,16,128]{2,0,1:T(8,128)(2,1)}, u32[]{:S(2)}) copy-start(bf16[64,16,128]{2,0,1:T(8,128)(2,1)} %copy_bitcast_fusion.2) | copy-start | bytes 786436
  151.1 15.1 %all-to-all-start.2 = ((f32[2,8,20,128]{3,0,2,1:T(2,128)}), f32[2,8,20,128]{3,0,2,1:T(2,128)S(1)}, u32[]{:S(2)}, u32[]{:S(2)}) async-start(f32[2,8,20,128]{3,0,2,1:T(2,128)} %bitcast.88), calls=%async_computation.2 | async-start | bytes 327680 | tf_op jit(solution)/shard_map/all_to_all | solution.py:57
  157.9 8.4 %copy-start.1 = (f32[512,2,160]{0,2,1:T(8,128)S(1)}, f32[512,2,160]{0,2,1:T(8,128)}, u32[]{:S(2)}) copy-start(f32[512,2,160]{0,2,1:T(8,128)} %convolution_multiply_fusion) | copy-start | bytes 1966084
  162.2 18.0 %copy-start.2 = (bf16[512,16,128]{2,0,1:T(8,128)(2,1)S(1)}, bf16[512,16,128]{2,0,1:T(8,128)(2,1)}, u32[]{:S(2)}) copy-start(bf16[512,16,128]{2,0,1:T(8,128)(2,1)} %copy.109) | copy-start | bytes 6291460
  162.2 18.0 %copy-start.6 = (bf16[64,16,128]{2,0,1:T(8,128)(2,1)S(1)}, bf16[64,16,128]{2,0,1:T(8,128)(2,1)}, u32[]{:S(2)}) copy-start(bf16[64,16,128]{2,0,1:T(8,128)(2,1)} %copy_bitcast_fusion.1) | copy-start | bytes 786436
  169.2 17.5 %all-to-all-start.3 = ((bf16[8,64,256]{2,1,0:T(8,128)(2,1)}), bf16[8,64,256]{2,1,0:T(8,128)(2,1)S(1)}, u32[]{:S(2)}, u32[]{:S(2)}) async-start(bf16[8,64,256]{2,1,0:T(8,128)(2,1)} %reshape.179), calls=%async_computation.3 | async-start | bytes 524288 | tf_op jit(solution)/shard_map/all_to_all | solution.py:105
where the time goes:
time: 189 us; the launch traced here: 187 us
  starting transfers between devices  81.4 us (43%)
  local copies, waits for them, and re-layouts  44.6 us (24%)
  blocking collectives  22 us (12%)
  waiting for transfers between devices  16.7 us (9%)
  matrix products  15.7 us (8%)
  other arithmetic  6.05 us (3%)
    ppermute x8, starting transfers between devices, passed_along(): return lax.ppermute(shard, axis, pairs)  33.6 us
    all_to_all x1, starting transfers between devices, groups_before(): held = lax.all_to_all(dealt, 'z', split_axis=1, concat_axis=1, tiled=True)  25.6 us
    all_gather x1, blocking collectives, groups_before(): along_y = lax.all_gather(line_total, 'y')  22 us
    ppermute x8, local copies, waits for them, and re-layouts, passed_along(): return lax.ppermute(shard, axis, pairs)  14.5 us
    all_to_all x1, starting transfers between devices, linear_heads(): back = lax.all_to_all(out, GROUP, split_axis=0, concat_axis=2, tiled=True)  10.9 us
    concatenate x1, local copies, waits for them, and re-layouts, shards(): earlier = jnp.concatenate(earlier, axis=1)  10.8 us
    all_to_all x1, starting transfers between devices, groups_before(): back = lax.all_to_all(prefix, 'z', split_axis=1, concat_axis=1, tiled=True)  6.74 us
    all_to_all x1, waiting for transfers between devices, linear_heads(): got = lax.all_to_all(packed, GROUP, split_axis=1, concat_axis=0, tiled=True)  5.46 us
  transfers between devices with their start and end apart: 12, of which 4 were waited for; matrix products, arithmetic and copies ran while one was open for 31% of the time, Pallas kernels for 0%

commit v1 on v0

--- a/solution.py
+++ b/solution.py
@@ -54,7 +54,15 @@
     y_before = jnp.arange(along_y.shape[0]) < lax.axis_index("y")
     lines_before = jnp.sum(jnp.where(y_before[:, None, None, None], along_y, 0.0), axis=0)
     prefix = running - held + lines_before[:, None]
-    back = lax.all_to_all(prefix, "z", split_axis=1, concat_axis=1, tiled=True)
+    back = jnp.concatenate(
+        jax.lax.all_to_all(
+            jnp.stack(jnp.split(prefix, jax.lax.axis_size("z"), axis=1)),
+            "z",
+            split_axis=0,
+            concat_axis=0,
+        ),
+        axis=1,
+    )
     return back.reshape(heads, feats, width)
 
 

time: 189 us -> 194 us (1.026)
  local copies, waits for them, and re-layouts: 44.6 us -> 49.4 us
    unnamed x25 -> x32, local copies, waits for them, and re-layouts: 2.52 us -> 6.74 us
  transfers between devices with their start and end apart: 12 -> 12, of which waited for: 4 -> 4; matrix products, arithmetic and copies ran while one was open for 31% -> 30% of each run, Pallas kernels for 0% -> 0%
where the time goes in v1:
time: 194 us; the launch traced here: 192 us
  starting transfers between devices  81.4 us (42%)
  local copies, waits for them, and re-layouts  49.4 us (25%)
  blocking collectives  22 us (11%)
  waiting for transfers between devices  16.7 us (9%)
  matrix products  15.7 us (8%)
  other arithmetic  5.38 us (3%)
    ppermute x8, starting transfers between devices, passed_along(): return lax.ppermute(shard, axis, pairs)  33.6 us
    all_to_all x1, starting transfers between devices, groups_before(): held = lax.all_to_all(dealt, 'z', split_axis=1, concat_axis=1, tiled=True)  25.6 us
    all_gather x1, blocking collectives, groups_before(): along_y = lax.all_gather(line_total, 'y')  22 us
    ppermute x8, local copies, waits for them, and re-layouts, passed_along(): return lax.ppermute(shard, axis, pairs)  14.5 us
    all_to_all x1, starting transfers between devices, linear_heads(): back = lax.all_to_all(out, GROUP, split_axis=0, concat_axis=2, tiled=True)  10.9 us
    concatenate x1, local copies, waits for them, and re-layouts, shards(): earlier = jnp.concatenate(earlier, axis=1)  10.8 us
    all_to_all x1, starting transfers between devices, groups_before(): jax.lax.all_to_all(jnp.stack(jnp.split(prefix, jax.lax.axis_size('z'), ax...  6.74 us
    unnamed x32, local copies, waits for them, and re-layouts  6.74 us
  transfers between devices with their start and end apart: 12, of which 4 were waited for; matrix products, arithmetic and copies ran while one was open for 30% of the time, Pallas kernels for 0%

profile of v1, /device:TPU:1, one launch (start us, length us, event | category | flops | bytes accessed | tf_op | source)
XLA Modules:
  0.0 191.6 jit_solution(7137685744046331396)
XLA Ops:
  0.7 2.0 %pad_maximum_fusion = bf16[2,64,2048]{2,1,0:T(8,128)(2,1)} fusion(bf16[1,64,2048]{2,1,0:T(8,128)(2,1)} %bitcast.130, bf16[1,64,2048]{2,1,0:T(8,128)(2,1)} %bitcast.129), kind=kLoop, calls=%fused_computation.35 | loop fusion | flops 262144 | bytes 1048576 | tf_op jit(solution)/shard_map/stack | solution.py:129
  2.7 4.8 %collective-permute-start = (bf16[2,64,2048]{2,1,0:T(8,128)(2,1)}, bf16[2,64,2048]{2,1,0:T(8,128)(2,1)S(1)}, u32[]{:S(2)}, u32[]{:S(2)}) collective-permute-start(bf16[2,64,2048]{2,1,0:T(8,128)(2,1)} %pad_maximum_fusion), channel_id=1, source_target_pairs={{0,8},{1,9},{2,10},{3,11},{4,12},{5,13},{6,14},{7,15},{8,16},{9,17... | collective-permute-start | bytes 1572872 | tf_op jit(solution)/shard_map/ppermute | solution.py:33
  7.5 7.0 %collective-permute-start.1 = (bf16[2,64,2048]{2,1,0:T(8,128)(2,1)}, bf16[2,64,2048]{2,1,0:T(8,128)(2,1)S(1)}, u32[]{:S(2)}, u32[]{:S(2)}) collective-permute-start(bf16[2,64,2048]{2,1,0:T(8,128)(2,1)} %pad_maximum_fusion), channel_id=1, source_target_pairs={{0,7},{1,8},{2,9},{3,10},{4,11},{5,12},{6,13},{7,14},{8,15},{9,16}... | collective-permute-start | bytes 1572872 | tf_op jit(solution)/shard_map/ppermute | solution.py:33
  14.6 4.5 %collective-permute-start.2 = (bf16[2,64,2048]{2,1,0:T(8,128)(2,1)}, bf16[2,64,2048]{2,1,0:T(8,128)(2,1)S(1)}, u32[]{:S(2)}, u32[]{:S(2)}) collective-permute-start(bf16[2,64,2048]{2,1,0:T(8,128)(2,1)} %pad_maximum_fusion), channel_id=1, source_target_pairs={{0,6},{1,7},{2,8},{3,9},{4,10},{5,11},{6,12},{7,13},{8,14},{9,15},... | collective-permute-start | bytes 1572872 | tf_op jit(solution)/shard_map/ppermute | solution.py:33
  19.1 2.5 %collective-permute-start.3 = (bf16[2,64,2048]{2,1,0:T(8,128)(2,1)}, bf16[2,64,2048]{2,1,0:T(8,128)(2,1)}, u32[]{:S(2)}, u32[]{:S(2)}) collective-permute-start(bf16[2,64,2048]{2,1,0:T(8,128)(2,1)} %pad_maximum_fusion), channel_id=1, source_target_pairs={{0,5},{1,6},{2,7},{3,8},{4,9},{5,10},{6,11},{7,12},{8,13},{9,14},{... | collective-permute-start | bytes 1572872 | tf_op jit(solution)/shard_map/ppermute | solution.py:33
  21.6 5.5 %collective-permute-start.4 = (bf16[2,64,2048]{2,1,0:T(8,128)(2,1)}, bf16[2,64,2048]{2,1,0:T(8,128)(2,1)}, u32[]{:S(2)}, u32[]{:S(2)}) collective-permute-start(bf16[2,64,2048]{2,1,0:T(8,128)(2,1)} %pad_maximum_fusion), channel_id=1, source_target_pairs={{0,4},{1,5},{2,6},{3,7},{4,8},{5,9},{6,10},{7,11},{8,12},{9,13},{1... | collective-permute-start | bytes 1572872 | tf_op jit(solution)/shard_map/ppermute | solution.py:33
  31.1 4.5 %all-to-all-start = ((bf16[64,8,320]{2,0,1:T(8,128)(2,1)}), bf16[64,8,320]{2,0,1:T(8,128)(2,1)S(1)}, u32[]{:S(2)}, u32[]{:S(2)}) async-start(bf16[64,8,320]{2,0,1:T(8,128)(2,1)} %pad_maximum_fusion.1), calls=%async_computation | async-start | bytes 786432 | tf_op jit(solution)/shard_map/all_to_all | solution.py:82
  38.1 5.5 %all-to-all-done = bf16[64,8,320]{2,0,1:T(8,128)(2,1)S(1)} async-done(((bf16[64,8,320]{2,0,1:T(8,128)(2,1)}), bf16[64,8,320]{2,0,1:T(8,128)(2,1)S(1)}, u32[]{:S(2)}, u32[]{:S(2)}) %all-to-all-start) | async-done | bytes 327712 | tf_op jit(solution)/shard_map/all_to_all | solution.py:82
  46.8 25.6 %all-to-all-start.1 = ((f32[2,8,20,128]{3,0,2,1:T(2,128)}), f32[2,8,20,128]{3,0,2,1:T(2,128)}, u32[]{:S(2)}, u32[]{:S(2)}) async-start(f32[2,8,20,128]{3,0,2,1:T(2,128)} %bitcast.12), calls=%async_computation.1 | async-start | bytes 327680 | tf_op jit(solution)/shard_map/all_to_all | solution.py:50
  73.8 1.9 %collective-permute-start.5 = (bf16[2,64,2048]{2,1,0:T(8,128)(2,1)}, bf16[2,64,2048]{2,1,0:T(8,128)(2,1)}, u32[]{:S(2)}, u32[]{:S(2)}) collective-permute-start(bf16[2,64,2048]{2,1,0:T(8,128)(2,1)} %pad_maximum_fusion), channel_id=1, source_target_pairs={{0,3},{1,4},{2,5},{3,6},{4,7},{5,8},{6,9},{7,10},{8,11},{9,12},{10... | collective-permute-start | bytes 1572872 | tf_op jit(solution)/shard_map/ppermute | solution.py:33
  75.7 1.9 %collective-permute-start.6 = (bf16[2,64,2048]{2,1,0:T(8,128)(2,1)}, bf16[2,64,2048]{2,1,0:T(8,128)(2,1)}, u32[]{:S(2)}, u32[]{:S(2)}) collective-permute-start(bf16[2,64,2048]{2,1,0:T(8,128)(2,1)} %pad_maximum_fusion), channel_id=1, source_target_pairs={{0,2},{1,3},{2,4},{3,5},{4,6},{5,7},{6,8},{7,9},{8,10},{9,11},{10,... | collective-permute-start | bytes 1572872 | tf_op jit(solution)/shard_map/ppermute | solution.py:33
  77.6 5.4 %collective-permute-start.7 = (bf16[2,64,2048]{2,1,0:T(8,128)(2,1)}, bf16[2,64,2048]{2,1,0:T(8,128)(2,1)}, u32[]{:S(2)}, u32[]{:S(2)}) collective-permute-start(bf16[2,64,2048]{2,1,0:T(8,128)(2,1)} %pad_maximum_fusion), channel_id=1, source_target_pairs={{0,1},{1,2},{2,3},{3,4},{4,5},{5,6},{6,7},{7,8},{8,9},{9,10},{10,1... | collective-permute-start | bytes 1572872 | tf_op jit(solution)/shard_map/ppermute | solution.py:33
  83.0 1.6 convolution_multiply_fusion
  84.6 2.6 %fusion.9 = f32[2,128,512]{2,1,0:T(8,128)} fusion(bf16[512,2,128]{0,2,1:T(8,128)(2,1)S(1)} %bitcast.132, f32[2,512,512]{2,1,0:T(8,128)S(1)} %fusion.83, pred[512,512]{1,0:T(8,128)(4,1)S(1)} %iota_compare_fusion), kind=kOutput, calls=%fused_computation.12 | convolution fusion | flops 808452096 | bytes 3145728 | tf_op jit(solution)/shard_map/hij,jhe->ihe/dot_general | solution.py:105
  89.7 2.4 %copy.112 = bf16[2,64,2048]{1,2,0:T(8,128)(2,1)} copy(bf16[2,64,2048]{2,1,0:T(8,128)(2,1)} %collective-permute-done.3) | data formatting | bytes 1048576 | tf_op jit(solution)/shard_map/ppermute | solution.py:33
  92.0 2.4 %copy.113 = bf16[2,64,2048]{1,2,0:T(8,128)(2,1)} copy(bf16[2,64,2048]{2,1,0:T(8,128)(2,1)} %collective-permute-done.4) | data formatting | bytes 1048576 | tf_op jit(solution)/shard_map/ppermute | solution.py:33
  94.4 3.7 %collective-permute-done.5 = bf16[2,64,2048]{2,1,0:T(8,128)(2,1)} collective-permute-done((bf16[2,64,2048]{2,1,0:T(8,128)(2,1)}, bf16[2,64,2048]{2,1,0:T(8,128)(2,1)}, u32[]{:S(2)}, u32[]{:S(2)}) %collective-permute-start.5) | collective-permute-done | bytes 524320 | tf_op jit(solution)/shard_map/ppermute | solution.py:33
  98.1 2.4 %copy.114 = bf16[2,64,2048]{1,2,0:T(8,128)(2,1)} copy(bf16[2,64,2048]{2,1,0:T(8,128)(2,1)} %collective-permute-done.5) | data formatting | bytes 1048576 | tf_op jit(solution)/shard_map/ppermute | solution.py:33
  100.5 2.4 %copy.115 = bf16[2,64,2048]{1,2,0:T(8,128)(2,1)} copy(bf16[2,64,2048]{2,1,0:T(8,128)(2,1)} %collective-permute-done.6) | data formatting | bytes 1048576 | tf_op jit(solution)/shard_map/ppermute | solution.py:33
  103.0 2.4 %copy.116 = bf16[2,64,2048]{1,2,0:T(8,128)(2,1)} copy(bf16[2,64,2048]{2,1,0:T(8,128)(2,1)} %collective-permute-done.7) | data formatting | bytes 1048576 | tf_op jit(solution)/shard_map/ppermute | solution.py:33
  105.4 10.8 %concatenate.31 = bf16[2,512,2048]{1,2,0:T(8,128)(2,1)} concatenate(bf16[2,64,2048]{1,2,0:T(8,128)(2,1)S(1)} %copy.109, bf16[2,64,2048]{1,2,0:T(8,128)(2,1)S(1)} %copy.110, bf16[2,64,2048]{1,2,0:T(8,128)(2,1)S(1)} %copy.111, bf16[2,64,2048]{1,2,0:T(8,128)(2,1)} %copy.112, bf16[2,64,2048]{1,2,0:T(8,128)(2,1)} %copy.113, bf16[2,64,2048]{1,2,0:T(8,128)(2,1)} %copy.114, ...), dimensions={1} | concatenate | bytes 8388608 | tf_op jit(solution)/shard_map/concatenate | solution.py:131
  116.1 3.9 %fusion.75 = (bf16[1,512,2048]{1,2,0:T(8,128)(2,1)}, bf16[1,512,2048]{1,2,0:T(8,128)(2,1)S(1)}) fusion(bf16[2,512,2048]{1,2,0:T(8,128)(2,1)} %concatenate.31), kind=kLoop, calls=%fused_computation.93 | loop fusion | bytes 8388608 | tf_op jit(solution)/shard_map/slice | solution.py:132
  120.0 3.9 %copy.119 = bf16[512,16,128]{2,0,1:T(8,128)(2,1)} copy(bf16[512,16,128]{0,2,1:T(8,128)(2,1)} %bitcast.124) | data formatting | bytes 4194304 | tf_op jit(solution)/shard_map/concatenate | solution.py:132
  124.0 2.4 %copy.117 = bf16[512,16,128]{2,0,1:T(8,128)(2,1)} copy(bf16[512,16,128]{0,2,1:T(8,128)(2,1)S(1)} %bitcast.123) | data formatting | bytes 4194304 | tf_op jit(solution)/shard_map/concatenate | solution.py:133
  127.3 22.0 %all-gather = f32[16,1,20,128]{3,1,2,0:T(1,128)S(1)} all-gather(f32[2,1,20,128]{3,1,2,0:T(1,128)S(1)} %copy.104), channel_id=2, replica_groups=mesh['y'=8,'z'=8,'core'=2,'sub'=4] {'y'}, dimensions={0}, use_global_device_ids=true | all-gather | bytes 184320 | tf_op jit(solution)/shard_map/all_gather | solution.py:53
  155.3 6.7 %all-to-all-start.2 = ((f32[8,2,1,20,128]{4,1,3,2,0:T(2,128)}), f32[8,2,1,20,128]{4,1,3,2,0:T(2,128)S(1)}, u32[]{:S(2)}, u32[]{:S(2)}) async-start(f32[8,2,1,20,128]{4,1,3,2,0:T(2,128)} %fusion.49), calls=%async_computation.2 | async-start | bytes 327680 | tf_op jit(solution)/shard_map/all_to_all | solution.py:58
  162.1 4.3 %fusion.77 = (f32[16,64]{1,0:T(8,128)S(1)}, f32[16,64,576]{2,1,0:T(8,128)}) fusion(pred[64,576]{1,0:T(8,128)(4,1)S(1)} %and_and_fusion, bf16[64,16,128]{2,0,1:T(8,128)(2,1)S(1)} %copy-done.7, bf16[512,16,128]{2,0,1:T(8,128)(2,1)} %copy.119, bf16[64,2048]{1,0:T(8,128)(2,1)S(1)} %copy-done), kind=kOutput, calls=%fused_computation.95 | convolution fusion | flops 158073408 | bytes 5021696 | tf_op jit(solution)/shard_map/sub | solution.py:149
  166.3 4.1 %all-to-all-done.2 = f32[8,2,1,20,128]{4,1,3,2,0:T(2,128)S(1)} async-done(((f32[8,2,1,20,128]{4,1,3,2,0:T(2,128)}), f32[8,2,1,20,128]{4,1,3,2,0:T(2,128)S(1)}, u32[]{:S(2)}, u32[]{:S(2)}) %all-to-all-start.2) | async-done | bytes 163872 | tf_op jit(solution)/shard_map/all_to_all | solution.py:58
  170.4 1.8 multiply_reduce_fusion
  173.4 10.9 %all-to-all-start.3 = ((bf16[8,64,256]{2,1,0:T(8,128)(2,1)}), bf16[8,64,256]{2,1,0:T(8,128)(2,1)S(1)}, u32[]{:S(2)}, u32[]{:S(2)}) async-start(bf16[8,64,256]{2,1,0:T(8,128)(2,1)} %reshape.179), calls=%async_computation.3 | async-start | bytes 524288 | tf_op jit(solution)/shard_map/all_to_all | solution.py:113
  184.3 2.4 %fusion.24 = bf16[16,8,8,128]{3,2,1,0:T(8,128)(2,1)S(1)} fusion(bf16[64,16,128]{2,0,1:T(8,128)(2,1)S(1)} %copy-done.6, bf16[512,16,128]{2,0,1:T(8,128)(2,1)S(1)} %copy-done.2, f32[16,64,576]{2,1,0:T(8,128)} %get-tuple-element.9, f32[16,64]{1,0:T(8,128)S(1)} %get-tuple-element.8), kind=kOutput, calls=%fused_computation.28 | convolution fusion | flops 157024256 | bytes 4984832 | tf_op jit(solution)/shard_map/hij,jhd->ihd/dot_general | solution.py:151
  187.4 3.4 %all-to-all-done.3 = bf16[8,64,256]{2,1,0:T(8,128)(2,1)S(1)} async-done(((bf16[8,64,256]{2,1,0:T(8,128)(2,1)}), bf16[8,64,256]{2,1,0:T(8,128)(2,1)S(1)}, u32[]{:S(2)}, u32[]{:S(2)}) %all-to-all-start.3) | async-done | bytes 262176 | tf_op jit(solution)/shard_map/all_to_all | solution.py:113
  (81 shorter events, 23.0 us)
Async XLA Ops:
  0.6 161.4 %copy-start = (bf16[64,2048]{1,0:T(8,128)(2,1)S(1)}, bf16[64,2048]{1,0:T(8,128)(2,1)}, u32[]{:S(2)}) copy-start(bf16[64,2048]{1,0:T(8,128)(2,1)} %param.15) | copy-start | bytes 786436
  0.6 35.0 %copy-start.3 = (bf16[64,2048]{1,0:T(8,128)(2,1)S(1)}, bf16[64,2048]{1,0:T(8,128)(2,1)}, u32[]{:S(2)}) copy-start(bf16[64,2048]{1,0:T(8,128)(2,1)} %param.16) | copy-start | bytes 786436
  0.7 36.7 %copy-start.4 = (bf16[64,2048]{1,0:T(8,128)(2,1)S(1)}, bf16[64,2048]{1,0:T(8,128)(2,1)}, u32[]{:S(2)}) copy-start(bf16[64,2048]{1,0:T(8,128)(2,1)} %param.17) | copy-start | bytes 786436
  2.7 71.1 %collective-permute-start = (bf16[2,64,2048]{2,1,0:T(8,128)(2,1)}, bf16[2,64,2048]{2,1,0:T(8,128)(2,1)S(1)}, u32[]{:S(2)}, u32[]{:S(2)}) collective-permute-start(bf16[2,64,2048]{2,1,0:T(8,128)(2,1)} %pad_maximum_fusion), channel_id=1, source_target_pairs={{0,8},{1,9},{2,10},{3,11},{4,12},{5,13},{6,14},{7,15},{8,16},{9,17... | collective-permute-start | bytes 1572872 | tf_op jit(solution)/shard_map/ppermute | solution.py:33
  7.5 68.2 %collective-permute-start.1 = (bf16[2,64,2048]{2,1,0:T(8,128)(2,1)}, bf16[2,64,2048]{2,1,0:T(8,128)(2,1)S(1)}, u32[]{:S(2)}, u32[]{:S(2)}) collective-permute-start(bf16[2,64,2048]{2,1,0:T(8,128)(2,1)} %pad_maximum_fusion), channel_id=1, source_target_pairs={{0,7},{1,8},{2,9},{3,10},{4,11},{5,12},{6,13},{7,14},{8,15},{9,16}... | collective-permute-start | bytes 1572872 | tf_op jit(solution)/shard_map/ppermute | solution.py:33
  14.6 63.1 %collective-permute-start.2 = (bf16[2,64,2048]{2,1,0:T(8,128)(2,1)}, bf16[2,64,2048]{2,1,0:T(8,128)(2,1)S(1)}, u32[]{:S(2)}, u32[]{:S(2)}) collective-permute-start(bf16[2,64,2048]{2,1,0:T(8,128)(2,1)} %pad_maximum_fusion), channel_id=1, source_target_pairs={{0,6},{1,7},{2,8},{3,9},{4,10},{5,11},{6,12},{7,13},{8,14},{9,15},... | collective-permute-start | bytes 1572872 | tf_op jit(solution)/shard_map/ppermute | solution.py:33
  19.1 70.6 %collective-permute-start.3 = (bf16[2,64,2048]{2,1,0:T(8,128)(2,1)}, bf16[2,64,2048]{2,1,0:T(8,128)(2,1)}, u32[]{:S(2)}, u32[]{:S(2)}) collective-permute-start(bf16[2,64,2048]{2,1,0:T(8,128)(2,1)} %pad_maximum_fusion), channel_id=1, source_target_pairs={{0,5},{1,6},{2,7},{3,8},{4,9},{5,10},{6,11},{7,12},{8,13},{9,14},{... | collective-permute-start | bytes 1572872 | tf_op jit(solution)/shard_map/ppermute | solution.py:33
  21.6 70.5 %collective-permute-start.4 = (bf16[2,64,2048]{2,1,0:T(8,128)(2,1)}, bf16[2,64,2048]{2,1,0:T(8,128)(2,1)}, u32[]{:S(2)}, u32[]{:S(2)}) collective-permute-start(bf16[2,64,2048]{2,1,0:T(8,128)(2,1)} %pad_maximum_fusion), channel_id=1, source_target_pairs={{0,4},{1,5},{2,6},{3,7},{4,8},{5,9},{6,10},{7,11},{8,12},{9,13},{1... | collective-permute-start | bytes 1572872 | tf_op jit(solution)/shard_map/ppermute | solution.py:33
  30.1 14.0 %copy-start.10 = (f32[17,160,1]{1,0,2:T(8,128)S(1)}, f32[17,160,1]{1,0,2:T(8,128)}, u32[]{:S(2)}) copy-start(f32[17,160,1]{1,0,2:T(8,128)} %constant.80) | copy-start | bytes 32644
  31.1 13.7 %copy-start.8 = (f32[17,160,1]{1,0,2:T(8,128)S(1)}, f32[17,160,1]{1,0,2:T(8,128)}, u32[]{:S(2)}) copy-start(f32[17,160,1]{1,0,2:T(8,128)} %constant.81) | copy-start | bytes 32644
  31.1 12.5 %all-to-all-start = ((bf16[64,8,320]{2,0,1:T(8,128)(2,1)}), bf16[64,8,320]{2,0,1:T(8,128)(2,1)S(1)}, u32[]{:S(2)}, u32[]{:S(2)}) async-start(bf16[64,8,320]{2,0,1:T(8,128)(2,1)} %pad_maximum_fusion.1), calls=%async_computation | async-start | bytes 786432 | tf_op jit(solution)/shard_map/all_to_all | solution.py:82
  43.9 28.6 %copy-start.9 = (f32[17,160,1]{1,0,2:T(8,128)S(1)}, f32[17,160,1]{1,0,2:T(8,128)}, u32[]{:S(2)}) copy-start(f32[17,160,1]{1,0,2:T(8,128)} %constant.82) | copy-start | bytes 32644
  46.8 79.5 %all-to-all-start.1 = ((f32[2,8,20,128]{3,0,2,1:T(2,128)}), f32[2,8,20,128]{3,0,2,1:T(2,128)}, u32[]{:S(2)}, u32[]{:S(2)}) async-start(f32[2,8,20,128]{3,0,2,1:T(2,128)} %bitcast.12), calls=%async_computation.1 | async-start | bytes 327680 | tf_op jit(solution)/shard_map/all_to_all | solution.py:50
  73.8 24.4 %collective-permute-start.5 = (bf16[2,64,2048]{2,1,0:T(8,128)(2,1)}, bf16[2,64,2048]{2,1,0:T(8,128)(2,1)}, u32[]{:S(2)}, u32[]{:S(2)}) collective-permute-start(bf16[2,64,2048]{2,1,0:T(8,128)(2,1)} %pad_maximum_fusion), channel_id=1, source_target_pairs={{0,3},{1,4},{2,5},{3,6},{4,7},{5,8},{6,9},{7,10},{8,11},{9,12},{10... | collective-permute-start | bytes 1572872 | tf_op jit(solution)/shard_map/ppermute | solution.py:33
  75.7 24.8 %collective-permute-start.6 = (bf16[2,64,2048]{2,1,0:T(8,128)(2,1)}, bf16[2,64,2048]{2,1,0:T(8,128)(2,1)}, u32[]{:S(2)}, u32[]{:S(2)}) collective-permute-start(bf16[2,64,2048]{2,1,0:T(8,128)(2,1)} %pad_maximum_fusion), channel_id=1, source_target_pairs={{0,2},{1,3},{2,4},{3,5},{4,6},{5,7},{6,8},{7,9},{8,10},{9,11},{10,... | collective-permute-start | bytes 1572872 | tf_op jit(solution)/shard_map/ppermute | solution.py:33
  77.6 9.5 %copy-start.5 = (bf16[2,64,2048]{2,1,0:T(8,128)(2,1)}, bf16[2,64,2048]{2,1,0:T(8,128)(2,1)S(1)}, u32[]{:S(2)}) copy-start(bf16[2,64,2048]{2,1,0:T(8,128)(2,1)S(1)} %collective-permute-done.2) | copy-start | bytes 1572868
  77.6 25.3 %collective-permute-start.7 = (bf16[2,64,2048]{2,1,0:T(8,128)(2,1)}, bf16[2,64,2048]{2,1,0:T(8,128)(2,1)}, u32[]{:S(2)}, u32[]{:S(2)}) collective-permute-start(bf16[2,64,2048]{2,1,0:T(8,128)(2,1)} %pad_maximum_fusion), channel_id=1, source_target_pairs={{0,1},{1,2},{2,3},{3,4},{4,5},{5,6},{6,7},{7,8},{8,9},{9,10},{10,1... | collective-permute-start | bytes 1572872 | tf_op jit(solution)/shard_map/ppermute | solution.py:33
  123.9 38.1 %copy-start.7 = (bf16[64,16,128]{2,0,1:T(8,128)(2,1)S(1)}, bf16[64,16,128]{2,0,1:T(8,128)(2,1)}, u32[]{:S(2)}) copy-start(bf16[64,16,128]{2,0,1:T(8,128)(2,1)} %copy_bitcast_fusion.2) | copy-start | bytes 786436
  155.3 15.1 %all-to-all-start.2 = ((f32[8,2,1,20,128]{4,1,3,2,0:T(2,128)}), f32[8,2,1,20,128]{4,1,3,2,0:T(2,128)S(1)}, u32[]{:S(2)}, u32[]{:S(2)}) async-start(f32[8,2,1,20,128]{4,1,3,2,0:T(2,128)} %fusion.49), calls=%async_computation.2 | async-start | bytes 327680 | tf_op jit(solution)/shard_map/all_to_all | solution.py:58
  162.1 8.4 %copy-start.1 = (f32[512,2,160]{0,2,1:T(8,128)S(1)}, f32[512,2,160]{0,2,1:T(8,128)}, u32[]{:S(2)}) copy-start(f32[512,2,160]{0,2,1:T(8,128)} %convolution_multiply_fusion) | copy-start | bytes 1966084
  166.3 18.0 %copy-start.2 = (bf16[512,16,128]{2,0,1:T(8,128)(2,1)S(1)}, bf16[512,16,128]{2,0,1:T(8,128)(2,1)}, u32[]{:S(2)}) copy-start(bf16[512,16,128]{2,0,1:T(8,128)(2,1)} %copy.117) | copy-start | bytes 6291460
  166.3 18.0 %copy-start.6 = (bf16[64,16,128]{2,0,1:T(8,128)(2,1)S(1)}, bf16[64,16,128]{2,0,1:T(8,128)(2,1)}, u32[]{:S(2)}) copy-start(bf16[64,16,128]{2,0,1:T(8,128)(2,1)} %copy_bitcast_fusion.1) | copy-start | bytes 786436
  173.4 17.5 %all-to-all-start.3 = ((bf16[8,64,256]{2,1,0:T(8,128)(2,1)}), bf16[8,64,256]{2,1,0:T(8,128)(2,1)S(1)}, u32[]{:S(2)}, u32[]{:S(2)}) async-start(bf16[8,64,256]{2,1,0:T(8,128)(2,1)} %reshape.179), calls=%async_computation.3 | async-start | bytes 524288 | tf_op jit(solution)/shard_map/all_to_all | solution.py:113
